TPU v7x, 256 devices: a whole 4x4x8 slice. The times are simulated.
256 devices in a mesh: tile: 16 (over z, x_lo), obj: 16 (over x_hi, y, core).
Axes of the slice: x: 4 (x_hi: 2, x_lo: 2; x = x_hi * 2 + x_lo), y: 4, z: 8, core: 2. Of those that a mesh axis runs over, the one named last changes fastest.
Arguments:
- adjoint_in: float32 [256, 2, 256, 1024], P('obj', None, 'tile'), may hold values from -6 to 6
- checkpoint_store: float32 [64, 2, 256, 1024], P('obj', None, 'tile'), may hold values from 1900 to 2500, as said below
- interval: int32 [1], replicated, may hold values from 0 to 63
- sea_mask: int32 [256, 1024], P('tile'), may hold values 0 or 1
- zonal_speed: float32 [256, 1024], P('tile'), may hold values from -0.45 to 0.45
- mixing: float32 [256, 1024], P('tile'), may hold values from 0.02 to 0.2
- piston: float32 [256, 32], P('tile'), may hold values from 0.1 to 0.9
- cell_area: float32 [256, 32], P('tile'), may hold values from 5 to 50
- region: int32 [256, 32], P('tile'), may hold values from 0 to 255
Outputs:
- adjoint_out: float32 [256, 2, 256, 1024], P('obj', None, 'tile')
Inputs may be any that keep to these rules, and one draw needn't show every extreme that they name: region numbers name objectives. `checkpoint_store`: dissolved carbon lies in 1900 to 2100 and alkalinity exceeds it by 200 to 400 in every cell.
All inputs are finite; a program needn't handle non-finite values. No bound on the sum of `sea_mask` on one device may be relied on, other than what follows from the above.
Results may differ from a plain program's by a relative error of at most 0.0003.
Values sent between devices are 32-bit elements; how exact they have to be, the bound alone decides.
No kernel may reach another device: no remote copies, remote signals or barrier semaphores. Data moves between devices by JAX's collectives and lax.ppermute only.
A program may use at most 64 MiB of HBM per device.

v0:
```python
import jax
import jax.numpy as jnp
from jax import lax
from jax.sharding import PartitionSpec as P

ROWS = 32
LEVELS = 32
NEWTON = 4
DISSOCIATION_ONE = 1400.0
DISSOCIATION_TWO = 1.1
BORATE_CONSTANT = 2.5
BORON_TOTAL = 416.0
AIR_CARBON = 14.0
START_HYDROGEN = 2.0
ROW_DIFFUSION = 0.1


def padded(cells, sides, width):
    for axis, dim in sides:
        count = lax.axis_size(axis)
        head = lax.slice_in_dim(cells, 0, width, axis=dim)
        tail = lax.slice_in_dim(cells, cells.shape[dim] - width, cells.shape[dim], axis=dim)
        cells = jnp.concatenate(
            [
                lax.ppermute(tail, axis, [(i, (i + 1) % count) for i in range(count)]),
                cells,
                lax.ppermute(head, axis, [((i + 1) % count, i) for i in range(count)]),
            ],
            axis=dim,
        )
    return cells


def spread(value, axis, source):
    kept = jnp.where(lax.axis_index(axis) == source, value, 0).astype(value.dtype)
    return lax.psum(kept, axis)


def chemistry(carbon, alkalinity, piston, surface_sea):
    hydrogen = jnp.full_like(carbon, START_HYDROGEN)
    for iteration in range(NEWTON):
        square = hydrogen * hydrogen
        denominator = square + DISSOCIATION_ONE * hydrogen + DISSOCIATION_ONE * DISSOCIATION_TWO
        carbonate = carbon * DISSOCIATION_ONE * (hydrogen + 2.0 * DISSOCIATION_TWO) / denominator
        borate = BORON_TOTAL * BORATE_CONSTANT / (hydrogen + BORATE_CONSTANT)
        derivative = -carbon * DISSOCIATION_ONE * (
            square + 4.0 * DISSOCIATION_TWO * hydrogen + DISSOCIATION_ONE * DISSOCIATION_TWO
        ) / (denominator * denominator) - borate / (hydrogen + BORATE_CONSTANT)
        hydrogen = hydrogen - (carbonate + borate - alkalinity) / derivative
    square = hydrogen * hydrogen
    denominator = square + DISSOCIATION_ONE * hydrogen + DISSOCIATION_ONE * DISSOCIATION_TWO
    dissolved = carbon * square / denominator
    return surface_sea * piston * (AIR_CARBON - dissolved)


def forward_shift(source, offset):
    padding = jnp.zeros(source.shape[:-1] + (offset,), source.dtype)
    return jnp.concatenate([source[..., offset:], padding], axis=-1)


def backward_shift(source, offset):
    padding = jnp.zeros(source.shape[:-1] + (offset,), source.dtype)
    return jnp.concatenate([padding, source[..., :-offset]], axis=-1)


def column_weights(sea_float, mixing):
    cell_index = jnp.arange(LEVELS * ROWS, dtype=jnp.int32)
    row_open = (cell_index % ROWS < ROWS - 1).astype(jnp.float32)
    level_open = (cell_index // ROWS < LEVELS - 1).astype(jnp.float32)
    row_weight = ROW_DIFFUSION * row_open * sea_float * forward_shift(sea_float, 1)
    level_weight = mixing * level_open * sea_float * forward_shift(sea_float, ROWS)
    return (row_weight, level_weight)


def column_mix(source, row_weight, level_weight):
    row_flux = row_weight * (forward_shift(source, 1) - source)
    level_flux = level_weight * (forward_shift(source, ROWS) - source)
    return row_flux - backward_shift(row_flux, 1) + level_flux - backward_shift(level_flux, ROWS)


def zonal_weights(sea_float, sea_east, velocity):
    opened = sea_float * sea_east
    magnitude = jnp.abs(velocity)
    return jnp.stack(
        [
            opened * (-velocity - magnitude) / 12.0,
            opened * (7.0 * velocity + 3.0 * magnitude) / 12.0,
            opened * (7.0 * velocity - 3.0 * magnitude) / 12.0,
            opened * (magnitude - velocity) / 12.0,
        ]
    )


def trim_rim(source, keep_rim, outer_rim, dimension):
    length = source.shape[dimension] - 2 * outer_rim
    return lax.slice_in_dim(
        source, outer_rim - keep_rim, outer_rim + length + keep_rim, axis=dimension
    )


def surface_slopes(carbon, alkalinity, piston, surface_sea):

    def uptake_of(carbon_in, alkalinity_in):
        return chemistry(carbon_in, alkalinity_in, piston, surface_sea)

    uptake, pullback = jax.vjp(uptake_of, carbon, alkalinity)
    by_carbon, by_alkalinity = pullback(jnp.ones_like(carbon))
    return (uptake, jnp.stack([by_carbon, by_alkalinity]))


def advance_rim(extended, weights, row_weight, level_weight, uptake):
    length = extended.shape[1]
    face_flux = (
        weights[0, 1 : length - 2] * extended[:, 0 : length - 3]
        + weights[1, 1 : length - 2] * extended[:, 1 : length - 2]
        + weights[2, 1 : length - 2] * extended[:, 2 : length - 1]
        + weights[3, 1 : length - 2] * extended[:, 3:length]
    )
    interior = extended[:, 2 : length - 2]
    zonal_term = -(face_flux[:, 1:] - face_flux[:, :-1])
    transported = interior + zonal_term + column_mix(interior, row_weight, level_weight)
    surface_row = transported[0, :, :ROWS] + uptake
    carbon = jnp.concatenate([surface_row, transported[0, :, ROWS:]], axis=-1)
    return jnp.stack([carbon, transported[1]])


def retreat(extended, weights, row_weight, level_weight, slopes, objective_seeds):
    length = extended.shape[2]
    difference = extended[:, :, 1:] - extended[:, :, :-1]
    zonal_term = (
        weights[0, 3 : length - 1] * difference[:, :, 3 : length - 1]
        + weights[1, 2 : length - 2] * difference[:, :, 2 : length - 2]
        + weights[2, 1 : length - 3] * difference[:, :, 1 : length - 3]
        + weights[3, 0 : length - 4] * difference[:, :, 0 : length - 4]
    )
    interior = extended[:, :, 2 : length - 2]
    adjoint = interior + zonal_term + column_mix(interior, row_weight, level_weight)
    forcing = interior[:, 0, :, :ROWS] + objective_seeds
    surface = adjoint[..., :ROWS] + slopes[None] * forcing[:, None]
    return jnp.concatenate([surface, adjoint[..., ROWS:]], axis=-1)


def body(
    adjoint_in, checkpoint_store, interval, sea_mask, zonal_speed, mixing, piston, cell_area, region
):
    groups = adjoint_in.shape[0]
    cell_count = adjoint_in.shape[3]
    rim_depth = 4
    statics = jnp.concatenate(
        [
            sea_mask.astype(jnp.float32),
            zonal_speed,
            mixing,
            piston,
            cell_area,
            region.astype(jnp.float32),
        ],
        axis=1,
    )
    widened = padded(statics, (("tile", 0),), rim_depth)
    sea_wide = widened[:, :cell_count]
    speed_wide = widened[:, cell_count : 2 * cell_count]
    mixing_wide = widened[:, 2 * cell_count : 3 * cell_count]
    offset = 3 * cell_count
    piston_wide = widened[:, offset : offset + ROWS]
    area_wide = widened[:, offset + ROWS : offset + 2 * ROWS]
    region_wide = widened[:, offset + 2 * ROWS : offset + 3 * ROWS]
    sea_east = jnp.concatenate([sea_wide[1:], jnp.zeros_like(sea_wide[:1])], axis=0)
    weights = zonal_weights(sea_wide, sea_east, speed_wide)
    row_weight, level_weight = column_weights(sea_wide, mixing_wide)
    surface_sea = sea_wide[:, :ROWS]
    targets = (lax.axis_index("obj") * groups + jnp.arange(groups, dtype=jnp.int32)).astype(
        jnp.float32
    )
    objective_seeds = area_wide[None] * (region_wide[None] == targets[:, None, None]).astype(
        jnp.float32
    )
    owners = lax.axis_size("obj")
    owner_index = interval[0] % owners
    band = 2 * ROWS
    stored = lax.dynamic_index_in_dim(checkpoint_store, interval[0] // owners, 0, keepdims=False)
    stored = spread(stored[:, :, :band], "obj", owner_index)
    initial_wide = padded(stored, (("tile", 1),), rim_depth)
    inner_rim = 2
    piston_inner = trim_rim(piston_wide, inner_rim, rim_depth, 0)
    sea_inner = trim_rim(surface_sea, inner_rim, rim_depth, 0)
    initial_inner = trim_rim(initial_wide, inner_rim, rim_depth, 1)
    uptake_first, slopes_first = surface_slopes(
        initial_inner[0, :, :ROWS], initial_inner[1, :, :ROWS], piston_inner, sea_inner
    )
    following = advance_rim(
        initial_wide,
        weights[:, :, :band],
        trim_rim(row_weight, inner_rim, rim_depth, 0)[:, :band],
        trim_rim(level_weight, inner_rim, rim_depth, 0)[:, :band],
        uptake_first,
    )
    _, slopes_second = surface_slopes(
        following[0, :, :ROWS], following[1, :, :ROWS], piston_inner, sea_inner
    )
    extended = padded(adjoint_in, (("tile", 2),), rim_depth)
    middle = retreat(
        extended,
        weights,
        trim_rim(row_weight, inner_rim, rim_depth, 0),
        trim_rim(level_weight, inner_rim, rim_depth, 0),
        slopes_second,
        trim_rim(objective_seeds, inner_rim, rim_depth, 1),
    )
    return retreat(
        middle,
        trim_rim(weights, inner_rim, rim_depth, 1),
        trim_rim(row_weight, 0, rim_depth, 0),
        trim_rim(level_weight, 0, rim_depth, 0),
        trim_rim(slopes_first, 0, inner_rim, 1),
        trim_rim(objective_seeds, 0, rim_depth, 1),
    )


def solution(mesh):
    placed = (
        P("obj", None, "tile", None),
        P("obj", None, "tile", None),
        P(),
        P("tile", None),
        P("tile", None),
        P("tile", None),
        P("tile", None),
        P("tile", None),
        P("tile", None),
    )
    return jax.shard_map(
        body, mesh=mesh, in_specs=placed, out_specs=P("obj", None, "tile", None), check_vma=False
    )
```

profile of v0, /device:TPU:1, one launch (start us, length us, event | category | flops | bytes accessed | tf_op | source)
XLA Modules:
  0.0 127.1 jit_solution(1453807047856551090)
XLA Ops:
  0.7 0.3 copy-done
  1.1 65.3 %psum.7 = f32[2,16,64]{2,1,0:T(8,128)S(1)} all-reduce(f32[2,16,64]{2,1,0:T(8,128)S(1)} %slice_select_fusion), channel_id=1, replica_groups=mesh['tile'=16,'obj'=16] {'obj'}, use_global_device_ids=true, to_apply=%region_0.1 | all-reduce | flops 2048 | bytes 16384 | tf_op jit(solution)/shard_map/psum | solution.py:36
  66.3 0.3 collective-permute-start.4
  66.7 5.3 %collective-permute-start.5 = (f32[2,4,64]{2,1,0:T(4,128)S(1)}, f32[2,4,64]{2,1,0:T(4,128)S(1)}, u32[]{:S(2)}, u32[]{:S(2)}) collective-permute-start(f32[2,4,64]{2,1,0:T(4,128)S(1)} %get-tuple-element.44), channel_id=1, source_target_pairs={{16,0},{32,16},{48,32},{64,48},{80,64},{96,80},{112,96},{128,112},... | collective-permute-start | bytes 6152 | tf_op jit(solution)/shard_map/ppermute | solution.py:27
  72.0 0.7 convert_element_type.25
  72.7 0.8 convert_element_type.24
  73.5 1.0 concatenate.67
  74.6 3.6 %collective-permute-start.3 = (f32[4,3168]{1,0:T(4,128)S(1)}, f32[4,3168]{1,0:T(4,128)S(1)}, u32[]{:S(2)}, u32[]{:S(2)}) collective-permute-start(f32[4,3168]{1,0:T(4,128)S(1)} %get-tuple-element.38), channel_id=1, source_target_pairs={{16,0},{32,16},{48,32},{64,48},{80,64},{96,80},{112,96},{128,112},... | collective-permute-start | bytes 152072 | tf_op jit(solution)/shard_map/ppermute | solution.py:27
  78.1 1.8 %fusion.65 = (f32[16,2,4,1024]{3,2,0,1:T(4,128)S(1)}, f32[16,2,4,1024]{3,2,0,1:T(4,128)S(1)}) fusion(f32[16,2,16,1024]{3,2,1,0:T(8,128)} %param.9), kind=kLoop, calls=%fused_computation.232 | loop fusion | bytes 2097152 | tf_op jit(solution)/shard_map/slice | solution.py:22
  80.1 3.6 %collective-permute-start.1 = (f32[16,2,4,1024]{3,2,0,1:T(4,128)S(1)}, f32[16,2,4,1024]{3,2,0,1:T(4,128)S(1)}, u32[]{:S(2)}, u32[]{:S(2)}) collective-permute-start(f32[16,2,4,1024]{3,2,0,1:T(4,128)S(1)} %get-tuple-element.29), channel_id=1, source_target_pairs={{16,0},{32,16},{48,32},{64,48},{80,64},{96,80},{112,96},{128,112},... | collective-permute-start | bytes 1572872 | tf_op jit(solution)/shard_map/ppermute | solution.py:27
  84.2 0.7 slice_bitcast_fusion.7
  84.9 0.7 slice_bitcast_fusion.5
  85.8 0.2 add_bitcast_fusion.1
  86.6 0.6 slice.448
  87.2 0.6 slice.450
  87.9 0.7 slice_bitcast_fusion.3
  88.5 0.7 slice_bitcast_fusion.1
  89.2 13.3 %collective-permute-done = f32[16,2,4,1024]{3,2,0,1:T(4,128)S(1)} collective-permute-done((f32[16,2,4,1024]{3,2,0,1:T(4,128)S(1)}, f32[16,2,4,1024]{3,2,0,1:T(4,128)S(1)}, u32[]{:S(2)}, u32[]{:S(2)}) %collective-permute-start) | collective-permute-done | bytes 524320 | tf_op jit(solution)/shard_map/ppermute | solution.py:25
  102.5 2.1 %collective-permute-done.1 = f32[16,2,4,1024]{3,2,0,1:T(4,128)S(1)} collective-permute-done((f32[16,2,4,1024]{3,2,0,1:T(4,128)S(1)}, f32[16,2,4,1024]{3,2,0,1:T(4,128)S(1)}, u32[]{:S(2)}, u32[]{:S(2)}) %collective-permute-start.1) | collective-permute-done | bytes 524320 | tf_op jit(solution)/shard_map/ppermute | solution.py:27
  104.7 0.5 pad_maximum_fusion
  105.2 1.2 slice.398
  106.4 0.5 slice_subtract_fusion
  106.9 2.9 %slice.403 = f32[16,2,20,992]{3,2,0,1:T(8,128)} slice(f32[16,2,24,1024]{3,2,0,1:T(8,128)S(1)} %pad_maximum_fusion), slice={[0:16], [0:2], [2:22], [32:1024]} | slice | bytes 5079040 | tf_op jit(solution)/shard_map/slice | solution.py:58
  109.8 4.3 %fusion.4 = (f32[16,2,20,1024]{3,2,0,1:T(8,128)S(1)}, f32[16,2,20,1024]{3,2,0,1:T(8,128)S(1)}, f32[16,2,20,1024]{3,2,0,1:T(8,128)S(1)}) fusion(f32[16,2,23,1024]{3,2,0,1:T(8,128)S(1)} %slice_subtract_fusion, f32[16,2,24,1024]{3,2,0,1:T(8,128)S(1)} %pad_maximum_fusion, f32[20,1024]{1,0:T(8,128)S(1)} %copy-done.3, f32[20,1024]{1,0:T(8,128)S(1)} %copy-done.4, ...), kind=kLoop, calls=%fused_computation.8 | loop fusion | flops 7864320 | bytes 26621440 | tf_op jit(solution)/shard_map/add | solution.py:137
  114.1 2.4 %copy_add_fusion = f32[16,2,20,1024]{3,2,1,0:T(8,128)S(1)} fusion(f32[16,2,20,1024]{3,2,0,1:T(8,128)S(1)} %get-tuple-element.25, f32[16,2,20,992]{3,2,0,1:T(8,128)S(1)} %bitcast.356, f32[16,2,20,1024]{3,2,0,1:T(8,128)S(1)} %get-tuple-element.27, f32[16,2,20,1024]{3,2,0,1:T(8,128)S(1)} %get-tuple-element.26, f32[16,2,20,1023]{3,2,0,1:T(8,128)S(1)} %bitcast.355), kind=kLoop, calls=%fused_computation.16 | loop fusion | flops 2621440 | bytes 15644160 | tf_op jit(solution)/shard_map/add | solution.py:137
  116.5 0.8 slice.451
  117.3 0.9 slice.433
  118.4 1.7 %fusion.1 = f32[16,2,19,1024]{3,2,1,0:T(8,128)S(1)} fusion(f32[16,2,20,32]{3,2,1,0:T(8,128)S(1)} %slice_add_fusion, f32[16,2,20,992]{3,2,1,0:T(8,128)S(1)} %slice.433), kind=kLoop, calls=%fused_computation.4 | loop fusion | flops 1867776 | bytes 5111808 | tf_op jit(solution)/shard_map/sub | solution.py:129
  120.2 1.9 %fusion.9 = (f32[16,2,16,1024]{3,2,1,0:T(8,128)S(1)}, f32[16,2,16,1024]{3,2,1,0:T(8,128)S(1)}) fusion(f32[16,2,20,992]{3,2,1,0:T(8,128)S(1)} %slice.433, f32[16,2,20,32]{3,2,1,0:T(8,128)S(1)} %slice_add_fusion, f32[16,1024]{1,0:T(8,128)S(1)} %copy-done.5, f32[16,2,16,992]{3,2,1,0:T(8,128)S(1)} %slice.451, f32[16,1024]{1,0:T(8,128)S(1)} %copy-done.6), kind=kLoop, calls=%fused_computation.24 | loop fusion | flops 5242880 | bytes 8978432 | tf_op jit(solution)/shard_map/mul | solution.py:76
  122.1 2.4 %fusion.12 = f32[16,2,16,1024]{3,2,1,0:T(8,128)S(1)} fusion(f32[16,2,19,1024]{3,2,1,0:T(8,128)S(1)} %fusion.1, f32[16,2,16,992]{3,2,1,0:T(8,128)S(1)} %bitcast.358, f32[16,2,16,1024]{3,2,1,0:T(8,128)S(1)} %get-tuple-element.24, f32[16,2,16,1024]{3,2,1,0:T(8,128)S(1)} %get-tuple-element.23, f32[16,2,16,1023]{3,2,1,0:T(8,128)S(1)} %bitcast.357, ...), kind=kLoop, calls=%fused_computation.29 | loop fusion | flops 6815744 | bytes 21690368 | tf_op jit(solution)/shard_map/add | solution.py:137
  124.6 0.6 slice.456
  125.2 1.9 %pad_maximum_fusion.1 = f32[16,2,16,1024]{3,2,1,0:T(8,128)} fusion(f32[16,2,16,992]{3,2,1,0:T(8,128)S(1)} %slice.456, f32[16,2,16,32]{3,2,1,0:T(8,128)S(1)} %slice_add_fusion.1), kind=kLoop, calls=%fused_computation.35 | loop fusion | flops 524288 | bytes 4194304 | tf_op jit(solution)/shard_map/concatenate | solution.py:140
  (65 shorter events, 1.8 us)
Async XLA Ops:
  0.0 1.1 copy-start
  66.3 13.7 %collective-permute-start.4 = (f32[2,4,64]{2,1,0:T(4,128)S(1)}, f32[2,4,64]{2,1,0:T(4,128)S(1)}, u32[]{:S(2)}, u32[]{:S(2)}) collective-permute-start(f32[2,4,64]{2,1,0:T(4,128)S(1)} %get-tuple-element.43), channel_id=1, source_target_pairs={{0,16},{16,32},{32,48},{48,64},{64,80},{80,96},{96,112},{112,128},... | collective-permute-start | bytes 6152 | tf_op jit(solution)/shard_map/ppermute | solution.py:25
  66.7 17.0 %collective-permute-start.5 = (f32[2,4,64]{2,1,0:T(4,128)S(1)}, f32[2,4,64]{2,1,0:T(4,128)S(1)}, u32[]{:S(2)}, u32[]{:S(2)}) collective-permute-start(f32[2,4,64]{2,1,0:T(4,128)S(1)} %get-tuple-element.44), channel_id=1, source_target_pairs={{16,0},{32,16},{48,32},{64,48},{80,64},{96,80},{112,96},{128,112},... | collective-permute-start | bytes 6152 | tf_op jit(solution)/shard_map/ppermute | solution.py:27
  74.5 9.4 %collective-permute-start.2 = (f32[4,3168]{1,0:T(4,128)S(1)}, f32[4,3168]{1,0:T(4,128)S(1)}, u32[]{:S(2)}, u32[]{:S(2)}) collective-permute-start(f32[4,3168]{1,0:T(4,128)S(1)} %get-tuple-element.37), channel_id=1, source_target_pairs={{0,16},{16,32},{32,48},{48,64},{64,80},{80,96},{96,112},{112,128},... | collective-permute-start | bytes 152072 | tf_op jit(solution)/shard_map/ppermute | solution.py:25
  74.6 9.3 %collective-permute-start.3 = (f32[4,3168]{1,0:T(4,128)S(1)}, f32[4,3168]{1,0:T(4,128)S(1)}, u32[]{:S(2)}, u32[]{:S(2)}) collective-permute-start(f32[4,3168]{1,0:T(4,128)S(1)} %get-tuple-element.38), channel_id=1, source_target_pairs={{16,0},{32,16},{48,32},{64,48},{80,64},{96,80},{112,96},{128,112},... | collective-permute-start | bytes 152072 | tf_op jit(solution)/shard_map/ppermute | solution.py:27
  79.9 22.6 %collective-permute-start = (f32[16,2,4,1024]{3,2,0,1:T(4,128)S(1)}, f32[16,2,4,1024]{3,2,0,1:T(4,128)S(1)}, u32[]{:S(2)}, u32[]{:S(2)}) collective-permute-start(f32[16,2,4,1024]{3,2,0,1:T(4,128)S(1)} %get-tuple-element.28), channel_id=1, source_target_pairs={{0,16},{16,32},{32,48},{48,64},{64,80},{80,96},{96,112},{112,128},... | collective-permute-start | bytes 1572872 | tf_op jit(solution)/shard_map/ppermute | solution.py:25
  80.1 24.6 %collective-permute-start.1 = (f32[16,2,4,1024]{3,2,0,1:T(4,128)S(1)}, f32[16,2,4,1024]{3,2,0,1:T(4,128)S(1)}, u32[]{:S(2)}, u32[]{:S(2)}) collective-permute-start(f32[16,2,4,1024]{3,2,0,1:T(4,128)S(1)} %get-tuple-element.29), channel_id=1, source_target_pairs={{16,0},{32,16},{48,32},{64,48},{80,64},{96,80},{112,96},{128,112},... | collective-permute-start | bytes 1572872 | tf_op jit(solution)/shard_map/ppermute | solution.py:27
  84.0 20.7 %copy-start.1 = (f32[16,2,16,1024]{3,2,1,0:T(8,128)S(1)}, f32[16,2,16,1024]{3,2,1,0:T(8,128)}, u32[]{:S(2)}) copy-start(f32[16,2,16,1024]{3,2,1,0:T(8,128)} %param.9) | copy-start | bytes 6291460
  106.9 2.9 %copy-start.2 = (f32[20,1024]{1,0:T(8,128)S(1)}, f32[20,1024]{1,0:T(8,128)}, u32[]{:S(2)}) copy-start(f32[20,1024]{1,0:T(8,128)} %get-tuple-element.52) | copy-start | bytes 245764
  106.9 2.9 %copy-start.3 = (f32[20,1024]{1,0:T(8,128)S(1)}, f32[20,1024]{1,0:T(8,128)}, u32[]{:S(2)}) copy-start(f32[20,1024]{1,0:T(8,128)} %get-tuple-element.45) | copy-start | bytes 245764
  106.9 2.9 %copy-start.4 = (f32[20,1024]{1,0:T(8,128)S(1)}, f32[20,1024]{1,0:T(8,128)}, u32[]{:S(2)}) copy-start(f32[20,1024]{1,0:T(8,128)} %get-tuple-element.46) | copy-start | bytes 245764
  118.3 1.8 %copy-start.5 = (f32[16,1024]{1,0:T(8,128)S(1)}, f32[16,1024]{1,0:T(8,128)}, u32[]{:S(2)}) copy-start(f32[16,1024]{1,0:T(8,128)} %slice.448) | copy-start | bytes 196612
  118.4 1.8 %copy-start.6 = (f32[16,1024]{1,0:T(8,128)S(1)}, f32[16,1024]{1,0:T(8,128)}, u32[]{:S(2)}) copy-start(f32[16,1024]{1,0:T(8,128)} %slice.450) | copy-start | bytes 196612
  120.1 1.9 %copy-start.7 = (f32[16,1024]{1,0:T(8,128)S(1)}, f32[16,1024]{1,0:T(8,128)}, u32[]{:S(2)}) copy-start(f32[16,1024]{1,0:T(8,128)} %get-tuple-element.55) | copy-start | bytes 196612
  120.1 1.9 %copy-start.8 = (f32[16,1024]{1,0:T(8,128)S(1)}, f32[16,1024]{1,0:T(8,128)}, u32[]{:S(2)}) copy-start(f32[16,1024]{1,0:T(8,128)} %get-tuple-element.56) | copy-start | bytes 196612
  120.2 1.9 %copy-start.9 = (f32[16,1024]{1,0:T(8,128)S(1)}, f32[16,1024]{1,0:T(8,128)}, u32[]{:S(2)}) copy-start(f32[16,1024]{1,0:T(8,128)} %get-tuple-element.47) | copy-start | bytes 196612
  120.2 1.9 %copy-start.10 = (f32[16,1024]{1,0:T(8,128)S(1)}, f32[16,1024]{1,0:T(8,128)}, u32[]{:S(2)}) copy-start(f32[16,1024]{1,0:T(8,128)} %get-tuple-element.48) | copy-start | bytes 196612
where the time goes:
time: 127 us
  blocking collectives  65.3 us (51%)
  other arithmetic  18.5 us (15%)
  waiting for transfers between devices  15.4 us (12%)
  local copies, waits for them, and re-layouts  13.8 us (11%)
  starting transfers between devices  12.9 us (10%)
    psum x1, blocking collectives, spread(): return lax.psum(kept, axis)  65.3 us
    ppermute x3, waiting for transfers between devices, padded(): lax.ppermute(tail, axis, [(i, (i + 1) % count) for i in range(count)])  13.3 us
    ppermute x3, starting transfers between devices, padded(): lax.ppermute(head, axis, [((i + 1) % count, i) for i in range(count)])  12.5 us
    add x3, other arithmetic, retreat(): interior + zonal_term + column_mix(interior, row_weight, level_weight)  9.16 us
    slice x7, local copies, waits for them, and re-layouts, forward_shift(): return jnp.concatenate([source[..., offset:], padding], axis=-1)  5.15 us
  transfers between devices with their start and end apart: 6, of which 2 were waited for; matrix products, arithmetic and copies ran while one was open for 8% of the time, Pallas kernels for 0%

commit v1 on v0

--- a/solution.py
+++ b/solution.py
@@ -33,7 +33,7 @@
 
 def spread(value, axis, source):
     kept = jnp.where(lax.axis_index(axis) == source, value, 0).astype(value.dtype)
-    return lax.psum(kept, axis)
+    return lax.all_gather(kept, axis).sum(axis=0)
 
 
 def chemistry(carbon, alkalinity, piston, surface_sea):

time: 127 us -> 88.8 us (0.70)
  blocking collectives: 65.3 us -> 25.6 us
  starting transfers between devices: 12.9 us -> 14.8 us
    psum x1 -> x0, blocking collectives: 65.3 us -> none  [spread(): return lax.psum(kept, axis)]
    all_gather x0 -> x1, blocking collectives: none -> 25.6 us  [spread(): return lax.all_gather(kept, axis).sum(axis=0)]
    ppermute x3, starting transfers between devices: 0.48 us -> 2.27 us  [padded(): lax.ppermute(tail, axis, [(i, (i + 1) % count) for i in range(count)])]
where the time goes in v1:
time: 88.8 us; the launch traced here: 88.6 us
  blocking collectives  25.6 us (29%)
  other arithmetic  18.6 us (21%)
  waiting for transfers between devices  14.9 us (17%)
  starting transfers between devices  14.8 us (17%)
  local copies, waits for them, and re-layouts  13.5 us (15%)
  between operations  1.12 us (1%)
    all_gather x1, blocking collectives, spread(): return lax.all_gather(kept, axis).sum(axis=0)  25.6 us
    ppermute x3, waiting for transfers between devices, padded(): lax.ppermute(tail, axis, [(i, (i + 1) % count) for i in range(count)])  12.7 us
    ppermute x3, starting transfers between devices, padded(): lax.ppermute(head, axis, [((i + 1) % count, i) for i in range(count)])  12.6 us
    add x3, other arithmetic, retreat(): interior + zonal_term + column_mix(interior, row_weight, level_weight)  9.16 us
    slice x7, local copies, waits for them, and re-layouts, forward_shift(): return jnp.concatenate([source[..., offset:], padding], axis=-1)  5.15 us
    ppermute x3, starting transfers between devices, padded(): lax.ppermute(tail, axis, [(i, (i + 1) % count) for i in range(count)])  2.27 us
    sub x2, other arithmetic, retreat(): difference = extended[:, :, 1:] - extended[:, :, :-1]  2.24 us
    ppermute x3, waiting for transfers between devices, padded(): lax.ppermute(head, axis, [((i + 1) % count, i) for i in range(count)])  2.23 us
  transfers between devices with their start and end apart: 6, of which 2 were waited for; matrix products, arithmetic and copies ran while one was open for 8% of the time, Pallas kernels for 0%

profile of v1, /device:TPU:1, one launch (start us, length us, event | category | flops | bytes accessed | tf_op | source)
XLA Modules:
  0.0 88.6 jit_solution(17942203938662435904)
XLA Ops:
  0.0 0.8 convert_element_type.25
  0.8 0.8 convert_element_type.24
  1.6 1.0 %concatenate.67 = f32[16,3168]{1,0:T(8,128)S(1)} concatenate(f32[16,1024]{1,0:T(8,128)S(1)} %convert_element_type.24, f32[16,1024]{1,0:T(8,128)} %param.13, f32[16,1024]{1,0:T(8,128)} %param.14, f32[16,32]{1,0:T(8,128)} %param.15, f32[16,32]{1,0:T(8,128)} %param.16, f32[16,32]{1,0:T(8,128)S(1)} %convert_element_type.25), dimensions={1} | concatenate | bytes 405504 | tf_op jit(solution)/shard_map/concatenate | solution.py:149
  2.6 2.1 %collective-permute-start.2 = (f32[4,3168]{1,0:T(4,128)S(1)}, f32[4,3168]{1,0:T(4,128)S(1)}, u32[]{:S(2)}, u32[]{:S(2)}) collective-permute-start(f32[4,3168]{1,0:T(4,128)S(1)} %get-tuple-element.37), channel_id=1, source_target_pairs={{0,16},{16,32},{32,48},{48,64},{64,80},{80,96},{96,112},{112,128},... | collective-permute-start | bytes 152072 | tf_op jit(solution)/shard_map/ppermute | solution.py:25
  4.7 5.4 %collective-permute-start.3 = (f32[4,3168]{1,0:T(4,128)S(1)}, f32[4,3168]{1,0:T(4,128)S(1)}, u32[]{:S(2)}, u32[]{:S(2)}) collective-permute-start(f32[4,3168]{1,0:T(4,128)S(1)} %get-tuple-element.38), channel_id=1, source_target_pairs={{16,0},{32,16},{48,32},{64,48},{80,64},{96,80},{112,96},{128,112},... | collective-permute-start | bytes 152072 | tf_op jit(solution)/shard_map/ppermute | solution.py:27
  10.8 25.6 %all-gather = f32[32,16,64]{2,1,0:T(8,128)S(1)} all-gather(f32[2,16,64]{2,1,0:T(8,128)S(1)} %slice_select_fusion), channel_id=2, replica_groups=mesh['tile'=16,'obj'=16] {'obj'}, dimensions={0}, use_global_device_ids=true | all-gather | bytes 139264 | tf_op jit(solution)/shard_map/all_gather | solution.py:36
  36.6 3.6 %collective-permute-start.5 = (f32[2,4,64]{2,1,0:T(4,128)S(1)}, f32[2,4,64]{2,1,0:T(4,128)S(1)}, u32[]{:S(2)}, u32[]{:S(2)}) collective-permute-start(f32[2,4,64]{2,1,0:T(4,128)S(1)} %get-tuple-element.44), channel_id=1, source_target_pairs={{16,0},{32,16},{48,32},{64,48},{80,64},{96,80},{112,96},{128,112},... | collective-permute-start | bytes 6152 | tf_op jit(solution)/shard_map/ppermute | solution.py:27
  40.1 1.8 %fusion.65 = (f32[16,2,4,1024]{3,2,0,1:T(4,128)S(1)}, f32[16,2,4,1024]{3,2,0,1:T(4,128)S(1)}) fusion(f32[16,2,16,1024]{3,2,1,0:T(8,128)} %param.9), kind=kLoop, calls=%fused_computation.232 | loop fusion | bytes 2097152 | tf_op jit(solution)/shard_map/slice | solution.py:22
  42.0 3.6 %collective-permute-start.1 = (f32[16,2,4,1024]{3,2,0,1:T(4,128)S(1)}, f32[16,2,4,1024]{3,2,0,1:T(4,128)S(1)}, u32[]{:S(2)}, u32[]{:S(2)}) collective-permute-start(f32[16,2,4,1024]{3,2,0,1:T(4,128)S(1)} %get-tuple-element.29), channel_id=1, source_target_pairs={{16,0},{32,16},{48,32},{64,48},{80,64},{96,80},{112,96},{128,112},... | collective-permute-start | bytes 1572872 | tf_op jit(solution)/shard_map/ppermute | solution.py:27
  46.2 0.7 slice_bitcast_fusion.7
  46.9 0.7 slice_bitcast_fusion.5
  47.8 0.2 add_bitcast_fusion.1
  48.1 0.2 add_bitcast_fusion.3
  48.6 0.6 slice.448
  49.2 0.6 slice.450
  49.9 0.7 slice_bitcast_fusion.3
  50.5 0.7 slice_bitcast_fusion.1
  51.2 12.7 %collective-permute-done = f32[16,2,4,1024]{3,2,0,1:T(4,128)S(1)} collective-permute-done((f32[16,2,4,1024]{3,2,0,1:T(4,128)S(1)}, f32[16,2,4,1024]{3,2,0,1:T(4,128)S(1)}, u32[]{:S(2)}, u32[]{:S(2)}) %collective-permute-start) | collective-permute-done | bytes 524320 | tf_op jit(solution)/shard_map/ppermute | solution.py:25
  63.9 2.2 %collective-permute-done.1 = f32[16,2,4,1024]{3,2,0,1:T(4,128)S(1)} collective-permute-done((f32[16,2,4,1024]{3,2,0,1:T(4,128)S(1)}, f32[16,2,4,1024]{3,2,0,1:T(4,128)S(1)}, u32[]{:S(2)}, u32[]{:S(2)}) %collective-permute-start.1) | collective-permute-done | bytes 524320 | tf_op jit(solution)/shard_map/ppermute | solution.py:27
  66.1 0.5 pad_maximum_fusion
  66.6 1.2 %slice.398 = f32[16,2,20,1023]{3,2,0,1:T(8,128)S(1)} slice(f32[16,2,24,1024]{3,2,0,1:T(8,128)S(1)} %pad_maximum_fusion), slice={[0:16], [0:2], [2:22], [1:1024]} | slice | bytes 5237760 | tf_op jit(solution)/shard_map/slice | solution.py:58
  67.8 0.5 slice_subtract_fusion
  68.4 2.9 %slice.403 = f32[16,2,20,992]{3,2,0,1:T(8,128)} slice(f32[16,2,24,1024]{3,2,0,1:T(8,128)S(1)} %pad_maximum_fusion), slice={[0:16], [0:2], [2:22], [32:1024]} | slice | bytes 5079040 | tf_op jit(solution)/shard_map/slice | solution.py:58
  71.3 4.3 %fusion.4 = (f32[16,2,20,1024]{3,2,0,1:T(8,128)S(1)}, f32[16,2,20,1024]{3,2,0,1:T(8,128)S(1)}, f32[16,2,20,1024]{3,2,0,1:T(8,128)S(1)}) fusion(f32[16,2,23,1024]{3,2,0,1:T(8,128)S(1)} %slice_subtract_fusion, f32[16,2,24,1024]{3,2,0,1:T(8,128)S(1)} %pad_maximum_fusion, f32[20,1024]{1,0:T(8,128)S(1)} %copy-done.3, f32[20,1024]{1,0:T(8,128)S(1)} %copy-done.4, ...), kind=kLoop, calls=%fused_computation.8 | loop fusion | flops 7864320 | bytes 26621440 | tf_op jit(solution)/shard_map/add | solution.py:137
  75.6 2.4 %copy_add_fusion = f32[16,2,20,1024]{3,2,1,0:T(8,128)S(1)} fusion(f32[16,2,20,1024]{3,2,0,1:T(8,128)S(1)} %get-tuple-element.25, f32[16,2,20,992]{3,2,0,1:T(8,128)S(1)} %bitcast.357, f32[16,2,20,1024]{3,2,0,1:T(8,128)S(1)} %get-tuple-element.27, f32[16,2,20,1024]{3,2,0,1:T(8,128)S(1)} %get-tuple-element.26, f32[16,2,20,1023]{3,2,0,1:T(8,128)S(1)} %bitcast.356), kind=kLoop, calls=%fused_computation.16 | loop fusion | flops 2621440 | bytes 15644160 | tf_op jit(solution)/shard_map/add | solution.py:137
  78.0 0.8 slice.451
  78.8 0.9 slice.433
  79.8 1.7 %fusion.1 = f32[16,2,19,1024]{3,2,1,0:T(8,128)S(1)} fusion(f32[16,2,20,32]{3,2,1,0:T(8,128)S(1)} %slice_add_fusion, f32[16,2,20,992]{3,2,1,0:T(8,128)S(1)} %slice.433), kind=kLoop, calls=%fused_computation.4 | loop fusion | flops 1867776 | bytes 5111808 | tf_op jit(solution)/shard_map/sub | solution.py:129
  81.6 1.9 %fusion.9 = (f32[16,2,16,1024]{3,2,1,0:T(8,128)S(1)}, f32[16,2,16,1024]{3,2,1,0:T(8,128)S(1)}) fusion(f32[16,2,20,992]{3,2,1,0:T(8,128)S(1)} %slice.433, f32[16,2,20,32]{3,2,1,0:T(8,128)S(1)} %slice_add_fusion, f32[16,1024]{1,0:T(8,128)S(1)} %copy-done.5, f32[16,2,16,992]{3,2,1,0:T(8,128)S(1)} %slice.451, f32[16,1024]{1,0:T(8,128)S(1)} %copy-done.6), kind=kLoop, calls=%fused_computation.24 | loop fusion | flops 5242880 | bytes 8978432 | tf_op jit(solution)/shard_map/mul | solution.py:76
  83.6 2.4 %fusion.12 = f32[16,2,16,1024]{3,2,1,0:T(8,128)S(1)} fusion(f32[16,2,19,1024]{3,2,1,0:T(8,128)S(1)} %fusion.1, f32[16,2,16,992]{3,2,1,0:T(8,128)S(1)} %bitcast.359, f32[16,2,16,1024]{3,2,1,0:T(8,128)S(1)} %get-tuple-element.24, f32[16,2,16,1024]{3,2,1,0:T(8,128)S(1)} %get-tuple-element.23, f32[16,2,16,1023]{3,2,1,0:T(8,128)S(1)} %bitcast.358, ...), kind=kLoop, calls=%fused_computation.29 | loop fusion | flops 6815744 | bytes 21690368 | tf_op jit(solution)/shard_map/add | solution.py:137
  86.0 0.6 slice.456
  86.7 1.9 %pad_maximum_fusion.1 = f32[16,2,16,1024]{3,2,1,0:T(8,128)} fusion(f32[16,2,16,992]{3,2,1,0:T(8,128)S(1)} %slice.456, f32[16,2,16,32]{3,2,1,0:T(8,128)S(1)} %slice_add_fusion.1), kind=kLoop, calls=%fused_computation.35 | loop fusion | flops 524288 | bytes 4194304 | tf_op jit(solution)/shard_map/concatenate | solution.py:140
  (66 shorter events, 1.6 us)
Async XLA Ops:
  0.0 10.8 %copy-start = (f32[4,2,16,1024]{3,2,1,0:T(8,128)S(1)}, f32[4,2,16,1024]{3,2,1,0:T(8,128)}, u32[]{:S(2)}) copy-start(f32[4,2,16,1024]{3,2,1,0:T(8,128)} %param.10) | copy-start | bytes 1572868
  2.6 43.2 %collective-permute-start.2 = (f32[4,3168]{1,0:T(4,128)S(1)}, f32[4,3168]{1,0:T(4,128)S(1)}, u32[]{:S(2)}, u32[]{:S(2)}) collective-permute-start(f32[4,3168]{1,0:T(4,128)S(1)} %get-tuple-element.37), channel_id=1, source_target_pairs={{0,16},{16,32},{32,48},{48,64},{64,80},{80,96},{96,112},{112,128},... | collective-permute-start | bytes 152072 | tf_op jit(solution)/shard_map/ppermute | solution.py:25
  4.7 41.1 %collective-permute-start.3 = (f32[4,3168]{1,0:T(4,128)S(1)}, f32[4,3168]{1,0:T(4,128)S(1)}, u32[]{:S(2)}, u32[]{:S(2)}) collective-permute-start(f32[4,3168]{1,0:T(4,128)S(1)} %get-tuple-element.38), channel_id=1, source_target_pairs={{16,0},{32,16},{48,32},{64,48},{80,64},{96,80},{112,96},{128,112},... | collective-permute-start | bytes 152072 | tf_op jit(solution)/shard_map/ppermute | solution.py:27
  36.5 5.6 %collective-permute-start.4 = (f32[2,4,64]{2,1,0:T(4,128)S(1)}, f32[2,4,64]{2,1,0:T(4,128)S(1)}, u32[]{:S(2)}, u32[]{:S(2)}) collective-permute-start(f32[2,4,64]{2,1,0:T(4,128)S(1)} %get-tuple-element.43), channel_id=1, source_target_pairs={{0,16},{16,32},{32,48},{48,64},{64,80},{80,96},{96,112},{112,128},... | collective-permute-start | bytes 6152 | tf_op jit(solution)/shard_map/ppermute | solution.py:25
  36.6 9.1 %collective-permute-start.5 = (f32[2,4,64]{2,1,0:T(4,128)S(1)}, f32[2,4,64]{2,1,0:T(4,128)S(1)}, u32[]{:S(2)}, u32[]{:S(2)}) collective-permute-start(f32[2,4,64]{2,1,0:T(4,128)S(1)} %get-tuple-element.44), channel_id=1, source_target_pairs={{16,0},{32,16},{48,32},{64,48},{80,64},{96,80},{112,96},{128,112},... | collective-permute-start | bytes 6152 | tf_op jit(solution)/shard_map/ppermute | solution.py:27
  41.9 22.0 %collective-permute-start = (f32[16,2,4,1024]{3,2,0,1:T(4,128)S(1)}, f32[16,2,4,1024]{3,2,0,1:T(4,128)S(1)}, u32[]{:S(2)}, u32[]{:S(2)}) collective-permute-start(f32[16,2,4,1024]{3,2,0,1:T(4,128)S(1)} %get-tuple-element.28), channel_id=1, source_target_pairs={{0,16},{16,32},{32,48},{48,64},{64,80},{80,96},{96,112},{112,128},... | collective-permute-start | bytes 1572872 | tf_op jit(solution)/shard_map/ppermute | solution.py:25
  42.0 24.1 %collective-permute-start.1 = (f32[16,2,4,1024]{3,2,0,1:T(4,128)S(1)}, f32[16,2,4,1024]{3,2,0,1:T(4,128)S(1)}, u32[]{:S(2)}, u32[]{:S(2)}) collective-permute-start(f32[16,2,4,1024]{3,2,0,1:T(4,128)S(1)} %get-tuple-element.29), channel_id=1, source_target_pairs={{16,0},{32,16},{48,32},{64,48},{80,64},{96,80},{112,96},{128,112},... | collective-permute-start | bytes 1572872 | tf_op jit(solution)/shard_map/ppermute | solution.py:27
  46.0 20.1 %copy-start.1 = (f32[16,2,16,1024]{3,2,1,0:T(8,128)S(1)}, f32[16,2,16,1024]{3,2,1,0:T(8,128)}, u32[]{:S(2)}) copy-start(f32[16,2,16,1024]{3,2,1,0:T(8,128)} %param.9) | copy-start | bytes 6291460
  68.3 2.9 %copy-start.2 = (f32[20,1024]{1,0:T(8,128)S(1)}, f32[20,1024]{1,0:T(8,128)}, u32[]{:S(2)}) copy-start(f32[20,1024]{1,0:T(8,128)} %get-tuple-element.52) | copy-start | bytes 245764
  68.3 2.9 %copy-start.3 = (f32[20,1024]{1,0:T(8,128)S(1)}, f32[20,1024]{1,0:T(8,128)}, u32[]{:S(2)}) copy-start(f32[20,1024]{1,0:T(8,128)} %get-tuple-element.45) | copy-start | bytes 245764
  68.4 2.9 %copy-start.4 = (f32[20,1024]{1,0:T(8,128)S(1)}, f32[20,1024]{1,0:T(8,128)}, u32[]{:S(2)}) copy-start(f32[20,1024]{1,0:T(8,128)} %get-tuple-element.46) | copy-start | bytes 245764
  79.8 1.8 %copy-start.5 = (f32[16,1024]{1,0:T(8,128)S(1)}, f32[16,1024]{1,0:T(8,128)}, u32[]{:S(2)}) copy-start(f32[16,1024]{1,0:T(8,128)} %slice.448) | copy-start | bytes 196612
  79.8 1.8 %copy-start.6 = (f32[16,1024]{1,0:T(8,128)S(1)}, f32[16,1024]{1,0:T(8,128)}, u32[]{:S(2)}) copy-start(f32[16,1024]{1,0:T(8,128)} %slice.450) | copy-start | bytes 196612
  81.6 1.9 %copy-start.7 = (f32[16,1024]{1,0:T(8,128)S(1)}, f32[16,1024]{1,0:T(8,128)}, u32[]{:S(2)}) copy-start(f32[16,1024]{1,0:T(8,128)} %get-tuple-element.55) | copy-start | bytes 196612
  81.6 1.9 %copy-start.8 = (f32[16,1024]{1,0:T(8,128)S(1)}, f32[16,1024]{1,0:T(8,128)}, u32[]{:S(2)}) copy-start(f32[16,1024]{1,0:T(8,128)} %get-tuple-element.56) | copy-start | bytes 196612
  81.6 1.9 %copy-start.9 = (f32[16,1024]{1,0:T(8,128)S(1)}, f32[16,1024]{1,0:T(8,128)}, u32[]{:S(2)}) copy-start(f32[16,1024]{1,0:T(8,128)} %get-tuple-element.47) | copy-start | bytes 196612
  81.6 1.9 %copy-start.10 = (f32[16,1024]{1,0:T(8,128)S(1)}, f32[16,1024]{1,0:T(8,128)}, u32[]{:S(2)}) copy-start(f32[16,1024]{1,0:T(8,128)} %get-tuple-element.48) | copy-start | bytes 196612
